TPU v7x, 256 devices: a whole 4x4x8 slice. The times are simulated.
256 devices in a mesh: tm: 16 (over y, x), space: 16 (over z, core).
Axes of the slice: x: 4, y: 4, z: 8, core: 2. Of those that a mesh axis runs over, the one named last changes fastest.
Arguments:
- stored: bfloat16 [16, 288, 128, 128], P('tm', None, 'space'), may hold values from -6 to 6
- snapshot: int32 [16, 256], P('tm'), may hold values from 0 to 287, as said below
- balance_coef: float32 [128, 128], P('space'), may hold values from 0.5 to 2
- sea_mask: int32 [128, 128], P('space'), may hold values 0 or 1
Outputs:
- merged_basis: bfloat16 [256, 3, 128, 128], P('tm', None, 'space')
Inputs may be any that keep to these rules, and one draw needn't show every extreme that they name: `snapshot`: the 256 indices of one group are distinct.
All inputs are finite; a program needn't handle non-finite values. No bound on the sum of `sea_mask` on one device may be relied on, other than what follows from the above.
Results may differ from a plain program's by a relative error of at most 0.04.
Values may be sent and summed in bfloat16 or wider, within the bound.
No kernel may reach another device: no remote copies, remote signals or barrier semaphores. Data moves between devices by JAX's collectives and lax.ppermute only.
A program may use at most 64 MiB of HBM per device.

v0:
```python
import jax
import jax.numpy as jnp
from jax import lax
from jax.sharding import PartitionSpec as P

inv_root2 = 0.7071067811865476


def gathered_total(shard, axis):
    return lax.all_gather(shard, axis).astype(jnp.float32).sum(0)


def with_halo(cells, sides, width):
    for axis, dim in sides:
        count = lax.axis_size(axis)
        ends = count - 1
        head = lax.slice_in_dim(cells, 0, width, axis=dim)
        tail = lax.slice_in_dim(cells, cells.shape[dim] - width, cells.shape[dim], axis=dim)
        cells = jnp.concatenate(
            [
                lax.ppermute(tail, axis, [(i, (i + 1) % count) for i in range(ends)]),
                cells,
                lax.ppermute(head, axis, [((i + 1) % count, i) for i in range(ends)]),
            ],
            axis=dim,
        )
    return cells


def from_partner(shard, axis, stride):
    return lax.ppermute(shard, axis, [(i, i ^ 1 << stride) for i in range(lax.axis_size(axis))])


def balance(padded, balance_coef, sea_float):
    center = padded[:, 1:-1, :]
    values = center.astype(jnp.float32)
    east_cells = jnp.roll(values, -1, axis=2)
    west_cells = jnp.roll(values, 1, axis=2)
    zonal_flow = (-balance_coef * sea_float * (east_cells - west_cells)).astype(jnp.bfloat16)
    wide = padded.astype(jnp.float32)
    merid_flow = (balance_coef * sea_float * (wide[:, 2:, :] - wide[:, :-2, :])).astype(
        jnp.bfloat16
    )
    return jnp.stack([center, zonal_flow, merid_flow], axis=1).reshape(center.shape[0], -1)


def stack_pair(own_basis, other_basis, level_idx):
    own_bit = lax.axis_index("tm") // 2**level_idx % 2
    upper_part = jnp.where(own_bit == 0, own_basis, other_basis)
    lower_part = jnp.where(own_bit == 0, other_basis, own_basis)
    return jnp.concatenate([upper_part, lower_part], axis=0)


def merge_pair(own_basis, other_basis, level_idx, last_level):
    stacked = stack_pair(own_basis, other_basis, level_idx)
    members = own_basis.shape[0]
    local_gram = jnp.dot(stacked, stacked.T, preferred_element_type=jnp.float32)
    local_mixed = (local_gram[:, :members] + local_gram[:, members:]) * inv_root2
    mixed_cols = lax.psum(local_mixed, "space")
    normal = jnp.dot(
        mixed_cols.T,
        mixed_cols,
        precision=lax.Precision.HIGHEST,
        preferred_element_type=jnp.float32,
    )
    factor_low = jnp.linalg.cholesky(normal)
    rotation = (
        jax.scipy.linalg.solve_triangular(factor_low, mixed_cols.T, lower=True) * inv_root2
    ).astype(jnp.bfloat16)
    if last_level:
        member_share = rotation.shape[0] // lax.axis_size("tm")
        rotation = lax.dynamic_slice_in_dim(
            rotation, lax.axis_index("tm") * member_share, member_share, 0
        )
    return jnp.dot(rotation, stacked, preferred_element_type=jnp.float32).astype(jnp.bfloat16)


def body(stored, snapshot, balance_coef, sea_mask):
    sea_float = sea_mask.astype(jnp.float32)
    mean_state = jnp.mean(stored[0].astype(jnp.float32), axis=0)
    picked = jnp.take(stored[0], snapshot[0], axis=0)
    anomaly = ((picked.astype(jnp.float32) - mean_state) * sea_float).astype(jnp.bfloat16)
    padded = with_halo(anomaly, (("space", 1),), 1)
    basis_now = balance(padded, balance_coef, sea_float)
    levels = lax.axis_size("tm").bit_length() - 1
    first_level = 0
    other_padded = from_partner(padded, "tm", 0)
    partner = balance(other_padded, balance_coef, sea_float)
    basis_now = merge_pair(basis_now, partner, 0, levels == 1)
    first_level = 1
    for level_idx in range(first_level, levels):
        partner = from_partner(basis_now, "tm", level_idx)
        basis_now = merge_pair(basis_now, partner, level_idx, level_idx == levels - 1)
    return basis_now.reshape(basis_now.shape[0], 3, stored.shape[2], stored.shape[3])


def solution(mesh):
    placed = (P("tm", None, "space", None), P("tm", None), P("space", None), P("space", None))
    return jax.shard_map(
        body, mesh=mesh, in_specs=placed, out_specs=P("tm", None, "space", None), check_vma=False
    )
```

profile of v0, /device:TPU:1, one launch (start us, length us, event | category | flops | bytes accessed | tf_op | source)
XLA Modules:
  0.0 906.1 jit_solution(1723753065468144391)
XLA Ops:
  10.0 1.9 gather_fusion
  12.4 5.1 collective-permute-start.1
  17.5 1.9 collective-permute-start
  33.1 7.0 collective-permute-done.2
  40.1 2.9 fusion.98
  50.9 2.4 fusion.13
  54.2 3.0 fusion.10
  57.6 1.8 copy.53
  59.5 1.9 copy.52
  61.3 3.8 fusion.3
  66.2 112.5 %all-reduce.6.cloned.1.call-done = f32[512,256]{1,0:T(8,128)} async-done(((f32[512,256]{1,0:T(8,128)}), f32[512,256]{1,0:T(8,128)}) %all-reduce.6.cloned.1.call-update) | async-done | bytes 524304 | tf_op jit(solution)/shard_map/psum | solution.py:59
  178.7 2.2 fusion.101
  181.2 11.7 %cholesky.214 = f32[128,128]{1,0:T(8,128)S(1)} custom-call(f32[128,128]{1,0:T(8,128)S(1)} %cholesky.346), custom_call_target="Cholesky" | custom-call | tf_op jit(solution)/shard_map/jit(cholesky)/cholesky | solution.py:66
  192.9 9.8 %custom-call.17 = f32[1,128,128]{1,2,0:T(8,128)S(1)} custom-call(f32[1,128,128]{2,1,0:T(8,128)S(1)} %get-tuple-element.118), custom_call_target="InvertDiagBlocksLowerTriangular" | custom-call | tf_op jit(solution)/shard_map/jit(cholesky)/cholesky | solution.py:66
  203.2 11.7 %cholesky.231 = f32[128,128]{1,0:T(8,128)S(1)} custom-call(f32[128,128]{1,0:T(8,128)S(1)} %convolution_subtract_fusion.7), custom_call_target="Cholesky" | custom-call | tf_op jit(solution)/shard_map/jit(cholesky)/cholesky | solution.py:66
  217.7 4.2 while.8
  221.8 19.7 %custom-call.18 = f32[2,128,128]{1,2,0:T(8,128)S(1)} custom-call(f32[2,128,128]{2,1,0:T(8,128)S(1)} %get-tuple-element.33), custom_call_target="InvertDiagBlocksLowerTriangular" | custom-call | tf_op jit(solution)/shard_map/jit(_solve_triangular)/triangular_solve | solution.py:68
  244.0 2.8 collective-permute-start.3
  246.8 34.2 %collective-permute-done.3 = bf16[256,3072]{1,0:T(8,128)(2,1)} collective-permute-done((bf16[256,3072]{1,0:T(8,128)(2,1)S(1)}, bf16[256,3072]{1,0:T(8,128)(2,1)}, u32[]{:S(2)}, u32[]{:S(2)}) %collective-permute-start.3) | collective-permute-done | bytes 1572896 | tf_op jit(solution)/shard_map/ppermute | solution.py:31
  281.0 2.1 broadcast_select_fusion.3
  286.3 110.5 %all-reduce.8.cloned.1.call-done = f32[512,256]{1,0:T(8,128)} async-done(((f32[512,256]{1,0:T(8,128)}), f32[512,256]{1,0:T(8,128)}) %all-reduce.8.cloned.1.call-update) | async-done | bytes 524304 | tf_op jit(solution)/shard_map/psum | solution.py:59
  396.8 2.2 fusion.102
  399.2 11.7 %cholesky.248 = f32[128,128]{1,0:T(8,128)S(1)} custom-call(f32[128,128]{1,0:T(8,128)S(1)} %cholesky.349), custom_call_target="Cholesky" | custom-call | tf_op jit(solution)/shard_map/jit(cholesky)/cholesky | solution.py:66
  411.0 9.8 %custom-call.19 = f32[1,128,128]{1,2,0:T(8,128)S(1)} custom-call(f32[1,128,128]{2,1,0:T(8,128)S(1)} %get-tuple-element.114), custom_call_target="InvertDiagBlocksLowerTriangular" | custom-call | tf_op jit(solution)/shard_map/jit(cholesky)/cholesky | solution.py:66
  421.3 11.7 %cholesky.265 = f32[128,128]{1,0:T(8,128)S(1)} custom-call(f32[128,128]{1,0:T(8,128)S(1)} %convolution_subtract_fusion.6), custom_call_target="Cholesky" | custom-call | tf_op jit(solution)/shard_map/jit(cholesky)/cholesky | solution.py:66
  435.7 4.1 while.9
  439.8 19.7 %custom-call.20 = f32[2,128,128]{1,2,0:T(8,128)S(1)} custom-call(f32[2,128,128]{2,1,0:T(8,128)S(1)} %get-tuple-element.34), custom_call_target="InvertDiagBlocksLowerTriangular" | custom-call | tf_op jit(solution)/shard_map/jit(_solve_triangular)/triangular_solve | solution.py:68
  461.0 2.2 convolution_convert_fusion.1
  464.3 34.4 %collective-permute-done.4 = bf16[256,3072]{1,0:T(8,128)(2,1)} collective-permute-done((bf16[256,3072]{1,0:T(8,128)(2,1)}, bf16[256,3072]{1,0:T(8,128)(2,1)}, u32[]{:S(2)}, u32[]{:S(2)}) %collective-permute-start.4) | collective-permute-done | bytes 1572896 | tf_op jit(solution)/shard_map/ppermute | solution.py:31
  498.7 2.1 broadcast_select_fusion.5
  503.8 110.7 %all-reduce.10.cloned.1.call-done = f32[512,256]{1,0:T(8,128)} async-done(((f32[512,256]{1,0:T(8,128)}), f32[512,256]{1,0:T(8,128)}) %all-reduce.10.cloned.1.call-update) | async-done | bytes 524304 | tf_op jit(solution)/shard_map/psum | solution.py:59
  614.5 2.2 fusion.103
  617.0 11.7 %cholesky.282 = f32[128,128]{1,0:T(8,128)S(1)} custom-call(f32[128,128]{1,0:T(8,128)S(1)} %cholesky.352), custom_call_target="Cholesky" | custom-call | tf_op jit(solution)/shard_map/jit(cholesky)/cholesky | solution.py:66
  628.7 9.8 %custom-call.21 = f32[1,128,128]{1,2,0:T(8,128)S(1)} custom-call(f32[1,128,128]{2,1,0:T(8,128)S(1)} %get-tuple-element.110), custom_call_target="InvertDiagBlocksLowerTriangular" | custom-call | tf_op jit(solution)/shard_map/jit(cholesky)/cholesky | solution.py:66
  639.0 11.7 %cholesky.299 = f32[128,128]{1,0:T(8,128)S(1)} custom-call(f32[128,128]{1,0:T(8,128)S(1)} %convolution_subtract_fusion.5), custom_call_target="Cholesky" | custom-call | tf_op jit(solution)/shard_map/jit(cholesky)/cholesky | solution.py:66
  653.4 4.3 while.10
  657.8 19.7 %custom-call.22 = f32[2,128,128]{1,2,0:T(8,128)S(1)} custom-call(f32[2,128,128]{2,1,0:T(8,128)S(1)} %get-tuple-element.35), custom_call_target="InvertDiagBlocksLowerTriangular" | custom-call | tf_op jit(solution)/shard_map/jit(_solve_triangular)/triangular_solve | solution.py:68
  678.9 2.2 convolution_convert_fusion
  681.1 2.7 collective-permute-start.5
  683.8 34.4 %collective-permute-done.5 = bf16[256,3072]{1,0:T(8,128)(2,1)} collective-permute-done((bf16[256,3072]{1,0:T(8,128)(2,1)}, bf16[256,3072]{1,0:T(8,128)(2,1)}, u32[]{:S(2)}, u32[]{:S(2)}) %collective-permute-start.5) | collective-permute-done | bytes 1572896 | tf_op jit(solution)/shard_map/ppermute | solution.py:31
  718.2 2.1 broadcast_select_fusion.7
  723.0 111.0 %all-reduce.12.cloned.1.call-done = f32[512,256]{1,0:T(8,128)} async-done(((f32[512,256]{1,0:T(8,128)}), f32[512,256]{1,0:T(8,128)}) %all-reduce.12.cloned.1.call-update) | async-done | bytes 524304 | tf_op jit(solution)/shard_map/psum | solution.py:59
  834.0 2.2 fusion.104
  836.4 11.7 %cholesky.316 = f32[128,128]{1,0:T(8,128)S(1)} custom-call(f32[128,128]{1,0:T(8,128)S(1)} %cholesky.355), custom_call_target="Cholesky" | custom-call | tf_op jit(solution)/shard_map/jit(cholesky)/cholesky | solution.py:66
  848.2 9.8 %custom-call.23 = f32[1,128,128]{1,2,0:T(8,128)S(1)} custom-call(f32[1,128,128]{2,1,0:T(8,128)S(1)} %get-tuple-element.106), custom_call_target="InvertDiagBlocksLowerTriangular" | custom-call | tf_op jit(solution)/shard_map/jit(cholesky)/cholesky | solution.py:66
  858.5 11.9 %cholesky.333 = f32[128,128]{1,0:T(8,128)S(1)} custom-call(f32[128,128]{1,0:T(8,128)S(1)} %convolution_subtract_fusion.4), custom_call_target="Cholesky" | custom-call | tf_op jit(solution)/shard_map/jit(cholesky)/cholesky | solution.py:66
  873.0 3.9 while.11
  877.0 19.7 %custom-call.24 = f32[2,128,128]{1,2,0:T(8,128)S(1)} custom-call(f32[2,128,128]{2,1,0:T(8,128)S(1)} %get-tuple-element.36), custom_call_target="InvertDiagBlocksLowerTriangular" | custom-call | tf_op jit(solution)/shard_map/jit(_solve_triangular)/triangular_solve | solution.py:68
  (177 shorter events, 69.9 us)
Async XLA Ops:
  6.5 172.2 %all-reduce.6.cloned.1.call-start = ((), (), s32[]{:S(2)}) async-start(), calls=%async_computation | async-start | bytes 1048576 | tf_op jit(solution)/shard_map/psum | solution.py:59
  11.9 8.1 copy-start
  12.4 7.6 collective-permute-start.1
  17.5 3.9 collective-permute-start
  23.0 17.1 %collective-permute-start.2 = (bf16[256,10,128]{2,0,1:T(8,128)(2,1)}, bf16[256,10,128]{2,0,1:T(8,128)(2,1)}, u32[]{:S(2)}, u32[]{:S(2)}) collective-permute-start(bf16[256,10,128]{2,0,1:T(8,128)(2,1)} %copy.45), channel_id=1, source_target_pairs={{0,16},{16,0},{32,48},{48,32},{64,80},{80,64},{96,112},{112,96},{1... | collective-permute-start | bytes 1966088 | tf_op jit(solution)/shard_map/ppermute | solution.py:31
  27.1 4.3 copy-start.20
  27.1 4.3 copy-start.21
  50.9 2.4 copy-start.1
  50.9 2.4 copy-start.6
  50.9 2.6 copy-start.7
  50.9 2.9 copy-start.8
  50.9 3.3 copy-start.9
  54.2 3.0 copy-start.10
  59.5 1.9 copy-start.11
  66.0 330.8 %all-reduce.8.cloned.1.call-start = ((), (), s32[]{:S(2)}) async-start(), calls=%async_computation.1 | async-start | bytes 1048576 | tf_op jit(solution)/shard_map/psum | solution.py:59
  181.1 60.4 %copy-start.3 = (f32[512,256]{1,0:T(8,128)S(1)}, f32[512,256]{1,0:T(8,128)}, u32[]{:S(2)}) copy-start(f32[512,256]{1,0:T(8,128)} %all-reduce.6.cloned.1.call-done) | copy-start | bytes 1572868
  241.5 1.5 copy-start.12
  244.0 2.8 copy-start.19
  244.0 37.0 %collective-permute-start.3 = (bf16[256,3072]{1,0:T(8,128)(2,1)S(1)}, bf16[256,3072]{1,0:T(8,128)(2,1)}, u32[]{:S(2)}, u32[]{:S(2)}) collective-permute-start(bf16[256,3072]{1,0:T(8,128)(2,1)S(1)} %convolution_convert_fusion.2), channel_id=1, source_target_pairs={{0,32},{16,48},{32,0},{48,16},{64,96},{80,112},{96,64},{112,80},{1... | collective-permute-start | bytes 4718600 | tf_op jit(solution)/shard_map/ppermute | solution.py:31
  283.1 1.8 copy-start.15
  285.8 328.7 %all-reduce.10.cloned.1.call-start = ((), (), s32[]{:S(2)}) async-start(), calls=%async_computation.2 | async-start | bytes 1048576 | tf_op jit(solution)/shard_map/psum | solution.py:59
  399.2 60.3 %copy-start.4 = (f32[512,256]{1,0:T(8,128)S(1)}, f32[512,256]{1,0:T(8,128)}, u32[]{:S(2)}) copy-start(f32[512,256]{1,0:T(8,128)} %all-reduce.8.cloned.1.call-done) | copy-start | bytes 1572868
  459.5 1.5 copy-start.16
  463.1 35.6 %collective-permute-start.4 = (bf16[256,3072]{1,0:T(8,128)(2,1)}, bf16[256,3072]{1,0:T(8,128)(2,1)}, u32[]{:S(2)}, u32[]{:S(2)}) collective-permute-start(bf16[256,3072]{1,0:T(8,128)(2,1)} %convolution_convert_fusion.1), channel_id=1, source_target_pairs={{0,64},{16,80},{32,96},{48,112},{64,0},{80,16},{96,32},{112,48},{1... | collective-permute-start | bytes 4718600 | tf_op jit(solution)/shard_map/ppermute | solution.py:31
  500.8 1.8 copy-start.17
  503.6 330.4 %all-reduce.12.cloned.1.call-start = ((), (), s32[]{:S(2)}) async-start(), calls=%async_computation.3 | async-start | bytes 1048576 | tf_op jit(solution)/shard_map/psum | solution.py:59
  616.9 60.5 %copy-start.5 = (f32[512,256]{1,0:T(8,128)S(1)}, f32[512,256]{1,0:T(8,128)}, u32[]{:S(2)}) copy-start(f32[512,256]{1,0:T(8,128)} %all-reduce.10.cloned.1.call-done) | copy-start | bytes 1572868
  677.4 1.5 copy-start.18
  681.1 37.1 %collective-permute-start.5 = (bf16[256,3072]{1,0:T(8,128)(2,1)}, bf16[256,3072]{1,0:T(8,128)(2,1)}, u32[]{:S(2)}, u32[]{:S(2)}) collective-permute-start(bf16[256,3072]{1,0:T(8,128)(2,1)} %convolution_convert_fusion), channel_id=1, source_target_pairs={{0,128},{16,144},{32,160},{48,176},{64,192},{80,208},{96,224},{112... | collective-permute-start | bytes 4718600 | tf_op jit(solution)/shard_map/ppermute | solution.py:31
  720.3 1.8 copy-start.13
  836.4 60.3 %copy-start.2 = (f32[512,256]{1,0:T(8,128)S(1)}, f32[512,256]{1,0:T(8,128)}, u32[]{:S(2)}) copy-start(f32[512,256]{1,0:T(8,128)} %all-reduce.12.cloned.1.call-done) | copy-start | bytes 1572868
  896.7 1.5 copy-start.14
Sparse Core Ops, SparseCore 0:
  66.1 112.5 all-reduce.5
  286.0 110.8 all-reduce.7
  503.7 110.8 all-reduce.9
  723.1 110.8 all-reduce.11
where the time goes:
time: 914 us; the launch traced here: 906 us
  waiting for transfers between devices  557 us (61%)
  other arithmetic  241 us (26%)
  local copies, waits for them, and re-layouts  40.6 us (4%)
  matrix products  31.5 us (3%)
  between operations  19.1 us (2%)
  starting transfers between devices  15.7 us (2%)
    psum x4, waiting for transfers between devices, merge_pair(): mixed_cols = lax.psum(local_mixed, 'space')  445 us
    another operation x28, other arithmetic, merge_pair(): factor_low = jnp.linalg.cholesky(normal)  139 us
    ppermute x4, waiting for transfers between devices, from_partner(): lax.ppermute(shard, axis, [(i, i ^ 1 << stride) for i in range(lax.axis_s...  110 us
    another operation x9, other arithmetic, merge_pair(): jax.scipy.linalg.solve_triangular(factor_low, mixed_cols.T, lower=True)  78.8 us
  transfers between devices with their start and end apart: 10, of which 10 were waited for; matrix products, arithmetic and copies ran while one was open for 1% of the time, Pallas kernels for 0%

commit v1 on v0

--- a/solution.py
+++ b/solution.py
@@ -4,6 +4,15 @@
 from jax.sharding import PartitionSpec as P
 
 inv_root2 = 0.7071067811865476
+
+
+def added_up(x, mesh_axis):
+    size = lax.axis_size(mesh_axis)
+    total, far = (x, 1)
+    while far < size:
+        total = total + lax.ppermute(total, mesh_axis, [(i, i ^ far) for i in range(size)])
+        far = 2 * far
+    return total
 
 
 def gathered_total(shard, axis):
@@ -56,7 +65,7 @@
     members = own_basis.shape[0]
     local_gram = jnp.dot(stacked, stacked.T, preferred_element_type=jnp.float32)
     local_mixed = (local_gram[:, :members] + local_gram[:, members:]) * inv_root2
-    mixed_cols = lax.psum(local_mixed, "space")
+    mixed_cols = added_up(local_mixed, "space")
     normal = jnp.dot(
         mixed_cols.T,
         mixed_cols,

time: 914 us -> 735 us (0.80)
  waiting for transfers between devices: 557 us -> 358 us
  starting transfers between devices: 15.7 us -> 51.8 us
  between operations: 19.1 us -> 6.54 us
    psum x4 -> x0, waiting for transfers between devices: 445 us -> none  [merge_pair(): mixed_cols = lax.psum(local_mixed, 'space')]
    ppermute x0 -> x16, waiting for transfers between devices: none -> 248 us  [added_up(): lax.ppermute(total, mesh_axis, [(i, i ^ far) for i in range(size)])]
    ppermute x0 -> x16, starting transfers between devices: none -> 36.7 us  [added_up(): lax.ppermute(total, mesh_axis, [(i, i ^ far) for i in range(size)])]
  transfers between devices with their start and end apart: 10 -> 22, of which waited for: 10 -> 22; matrix products, arithmetic and copies ran while one was open for 1% -> 1% of each run, Pallas kernels for 0% -> 0%
where the time goes in v1:
time: 735 us; the launch traced here: 725 us
  waiting for transfers between devices  358 us (49%)
  other arithmetic  240 us (33%)
  starting transfers between devices  51.8 us (7%)
  local copies, waits for them, and re-layouts  41.3 us (6%)
  matrix products  26.9 us (4%)
    ppermute x16, waiting for transfers between devices, added_up(): lax.ppermute(total, mesh_axis, [(i, i ^ far) for i in range(size)])  248 us
    another operation x28, other arithmetic, merge_pair(): factor_low = jnp.linalg.cholesky(normal)  139 us
    ppermute x4, waiting for transfers between devices, from_partner(): lax.ppermute(shard, axis, [(i, i ^ 1 << stride) for i in range(lax.axis_s...  108 us
    another operation x9, other arithmetic, merge_pair(): jax.scipy.linalg.solve_triangular(factor_low, mixed_cols.T, lower=True)  78.8 us
    ppermute x16, starting transfers between devices, added_up(): lax.ppermute(total, mesh_axis, [(i, i ^ far) for i in range(size)])  36.7 us
    another operation x29, local copies, waits for them, and re-layouts, merge_pair(): jax.scipy.linalg.solve_triangular(factor_low, mixed_cols.T, lower=True)  16.4 us
  transfers between devices with their start and end apart: 22, of which 22 were waited for; matrix products, arithmetic and copies ran while one was open for 1% of the time, Pallas kernels for 0%

profile of v1, /device:TPU:1, one launch (start us, length us, event | category | flops | bytes accessed | tf_op | source)
XLA Modules:
  0.0 725.4 jit_solution(9073866080178970670)
XLA Ops:
  5.9 5.1 collective-permute-start.1
  26.6 7.0 collective-permute-done.2
  33.5 2.9 fusion.110
  47.7 3.0 fusion.10
  54.9 3.8 fusion.3
  62.4 11.6 %collective-permute-done.4 = f32[512,256]{1,0:T(8,128)S(1)} collective-permute-done((f32[512,256]{1,0:T(8,128)S(1)}, f32[512,256]{1,0:T(8,128)S(1)}, u32[]{:S(2)}, u32[]{:S(2)}) %collective-permute-start.4) | collective-permute-done | bytes 524320 | tf_op jit(solution)/shard_map/ppermute | solution.py:13
  74.1 4.8 collective-permute-start.5
  78.9 22.7 %collective-permute-done.5 = f32[512,256]{1,0:T(8,128)S(1)} collective-permute-done((f32[512,256]{1,0:T(8,128)S(1)}, f32[512,256]{1,0:T(8,128)S(1)}, u32[]{:S(2)}, u32[]{:S(2)}) %collective-permute-start.5) | collective-permute-done | bytes 524320 | tf_op jit(solution)/shard_map/ppermute | solution.py:13
  101.7 4.7 collective-permute-start.6
  106.4 23.0 %collective-permute-done.6 = f32[512,256]{1,0:T(8,128)S(1)} collective-permute-done((f32[512,256]{1,0:T(8,128)S(1)}, f32[512,256]{1,0:T(8,128)S(1)}, u32[]{:S(2)}, u32[]{:S(2)}) %collective-permute-start.6) | collective-permute-done | bytes 524320 | tf_op jit(solution)/shard_map/ppermute | solution.py:13
  130.6 11.7 %cholesky.214 = f32[128,128]{1,0:T(8,128)S(1)} custom-call(f32[128,128]{1,0:T(8,128)S(1)} %cholesky.346), custom_call_target="Cholesky" | custom-call | tf_op jit(solution)/shard_map/jit(cholesky)/cholesky | solution.py:75
  142.4 9.8 %custom-call.17 = f32[1,128,128]{1,2,0:T(8,128)S(1)} custom-call(f32[1,128,128]{2,1,0:T(8,128)S(1)} %get-tuple-element.118), custom_call_target="InvertDiagBlocksLowerTriangular" | custom-call | tf_op jit(solution)/shard_map/jit(cholesky)/cholesky | solution.py:75
  152.7 11.7 %cholesky.231 = f32[128,128]{1,0:T(8,128)S(1)} custom-call(f32[128,128]{1,0:T(8,128)S(1)} %slice_subtract_fusion.13), custom_call_target="Cholesky" | custom-call | tf_op jit(solution)/shard_map/jit(cholesky)/cholesky | solution.py:75
  167.3 4.6 while.8
  171.8 19.7 %custom-call.18 = f32[2,128,128]{1,2,0:T(8,128)S(1)} custom-call(f32[2,128,128]{2,1,0:T(8,128)S(1)} %get-tuple-element.33), custom_call_target="InvertDiagBlocksLowerTriangular" | custom-call | tf_op jit(solution)/shard_map/jit(_solve_triangular)/triangular_solve | solution.py:77
  197.0 32.8 %collective-permute-done.7 = bf16[256,3072]{1,0:T(8,128)(2,1)} collective-permute-done((bf16[256,3072]{1,0:T(8,128)(2,1)S(1)}, bf16[256,3072]{1,0:T(8,128)(2,1)}, u32[]{:S(2)}, u32[]{:S(2)}) %collective-permute-start.7) | collective-permute-done | bytes 1572896 | tf_op jit(solution)/shard_map/ppermute | solution.py:40
  233.7 3.0 collective-permute-start.8
  238.5 13.1 %collective-permute-done.9 = f32[512,256]{1,0:T(8,128)S(1)} collective-permute-done((f32[512,256]{1,0:T(8,128)S(1)}, f32[512,256]{1,0:T(8,128)S(1)}, u32[]{:S(2)}, u32[]{:S(2)}) %collective-permute-start.9) | collective-permute-done | bytes 524320 | tf_op jit(solution)/shard_map/ppermute | solution.py:13
  254.5 22.7 %collective-permute-done.10 = f32[512,256]{1,0:T(8,128)S(1)} collective-permute-done((f32[512,256]{1,0:T(8,128)S(1)}, f32[512,256]{1,0:T(8,128)S(1)}, u32[]{:S(2)}, u32[]{:S(2)}) %collective-permute-start.10) | collective-permute-done | bytes 524320 | tf_op jit(solution)/shard_map/ppermute | solution.py:13
  277.3 3.7 collective-permute-start.11
  281.0 25.2 %collective-permute-done.11 = f32[512,256]{1,0:T(8,128)S(1)} collective-permute-done((f32[512,256]{1,0:T(8,128)S(1)}, f32[512,256]{1,0:T(8,128)S(1)}, u32[]{:S(2)}, u32[]{:S(2)}) %collective-permute-start.11) | collective-permute-done | bytes 524320 | tf_op jit(solution)/shard_map/ppermute | solution.py:13
  307.4 11.7 %cholesky.248 = f32[128,128]{1,0:T(8,128)S(1)} custom-call(f32[128,128]{1,0:T(8,128)S(1)} %cholesky.349), custom_call_target="Cholesky" | custom-call | tf_op jit(solution)/shard_map/jit(cholesky)/cholesky | solution.py:75
  319.1 9.8 %custom-call.19 = f32[1,128,128]{1,2,0:T(8,128)S(1)} custom-call(f32[1,128,128]{2,1,0:T(8,128)S(1)} %get-tuple-element.114), custom_call_target="InvertDiagBlocksLowerTriangular" | custom-call | tf_op jit(solution)/shard_map/jit(cholesky)/cholesky | solution.py:75
  329.4 11.7 %cholesky.265 = f32[128,128]{1,0:T(8,128)S(1)} custom-call(f32[128,128]{1,0:T(8,128)S(1)} %slice_subtract_fusion.12), custom_call_target="Cholesky" | custom-call | tf_op jit(solution)/shard_map/jit(cholesky)/cholesky | solution.py:75
  344.0 4.4 while.9
  348.3 19.7 %custom-call.20 = f32[2,128,128]{1,2,0:T(8,128)S(1)} custom-call(f32[2,128,128]{2,1,0:T(8,128)S(1)} %get-tuple-element.34), custom_call_target="InvertDiagBlocksLowerTriangular" | custom-call | tf_op jit(solution)/shard_map/jit(_solve_triangular)/triangular_solve | solution.py:77
  373.0 34.2 %collective-permute-done.12 = bf16[256,3072]{1,0:T(8,128)(2,1)} collective-permute-done((bf16[256,3072]{1,0:T(8,128)(2,1)}, bf16[256,3072]{1,0:T(8,128)(2,1)}, u32[]{:S(2)}, u32[]{:S(2)}) %collective-permute-start.12) | collective-permute-done | bytes 1572896 | tf_op jit(solution)/shard_map/ppermute | solution.py:40
  414.7 13.1 %collective-permute-done.14 = f32[512,256]{1,0:T(8,128)S(1)} collective-permute-done((f32[512,256]{1,0:T(8,128)S(1)}, f32[512,256]{1,0:T(8,128)S(1)}, u32[]{:S(2)}, u32[]{:S(2)}) %collective-permute-start.14) | collective-permute-done | bytes 524320 | tf_op jit(solution)/shard_map/ppermute | solution.py:13
  430.5 22.7 %collective-permute-done.15 = f32[512,256]{1,0:T(8,128)S(1)} collective-permute-done((f32[512,256]{1,0:T(8,128)S(1)}, f32[512,256]{1,0:T(8,128)S(1)}, u32[]{:S(2)}, u32[]{:S(2)}) %collective-permute-start.15) | collective-permute-done | bytes 524320 | tf_op jit(solution)/shard_map/ppermute | solution.py:13
  453.3 3.3 collective-permute-start.16
  456.7 25.9 %collective-permute-done.16 = f32[512,256]{1,0:T(8,128)S(1)} collective-permute-done((f32[512,256]{1,0:T(8,128)S(1)}, f32[512,256]{1,0:T(8,128)S(1)}, u32[]{:S(2)}, u32[]{:S(2)}) %collective-permute-start.16) | collective-permute-done | bytes 524320 | tf_op jit(solution)/shard_map/ppermute | solution.py:13
  483.8 11.7 %cholesky.282 = f32[128,128]{1,0:T(8,128)S(1)} custom-call(f32[128,128]{1,0:T(8,128)S(1)} %cholesky.352), custom_call_target="Cholesky" | custom-call | tf_op jit(solution)/shard_map/jit(cholesky)/cholesky | solution.py:75
  495.5 9.8 %custom-call.21 = f32[1,128,128]{1,2,0:T(8,128)S(1)} custom-call(f32[1,128,128]{2,1,0:T(8,128)S(1)} %get-tuple-element.110), custom_call_target="InvertDiagBlocksLowerTriangular" | custom-call | tf_op jit(solution)/shard_map/jit(cholesky)/cholesky | solution.py:75
  505.8 11.7 %cholesky.299 = f32[128,128]{1,0:T(8,128)S(1)} custom-call(f32[128,128]{1,0:T(8,128)S(1)} %slice_subtract_fusion.11), custom_call_target="Cholesky" | custom-call | tf_op jit(solution)/shard_map/jit(cholesky)/cholesky | solution.py:75
  520.4 4.3 while.10
  524.7 19.7 %custom-call.22 = f32[2,128,128]{1,2,0:T(8,128)S(1)} custom-call(f32[2,128,128]{2,1,0:T(8,128)S(1)} %get-tuple-element.35), custom_call_target="InvertDiagBlocksLowerTriangular" | custom-call | tf_op jit(solution)/shard_map/jit(_solve_triangular)/triangular_solve | solution.py:77
  548.1 2.9 collective-permute-start.17
  551.1 34.3 %collective-permute-done.17 = bf16[256,3072]{1,0:T(8,128)(2,1)} collective-permute-done((bf16[256,3072]{1,0:T(8,128)(2,1)}, bf16[256,3072]{1,0:T(8,128)(2,1)}, u32[]{:S(2)}, u32[]{:S(2)}) %collective-permute-start.17) | collective-permute-done | bytes 1572896 | tf_op jit(solution)/shard_map/ppermute | solution.py:40
  592.6 13.1 %collective-permute-done.19 = f32[512,256]{1,0:T(8,128)S(1)} collective-permute-done((f32[512,256]{1,0:T(8,128)S(1)}, f32[512,256]{1,0:T(8,128)S(1)}, u32[]{:S(2)}, u32[]{:S(2)}) %collective-permute-start.19) | collective-permute-done | bytes 524320 | tf_op jit(solution)/shard_map/ppermute | solution.py:13
  605.8 3.3 collective-permute-start.20
  609.1 22.7 %collective-permute-done.20 = f32[512,256]{1,0:T(8,128)S(1)} collective-permute-done((f32[512,256]{1,0:T(8,128)S(1)}, f32[512,256]{1,0:T(8,128)S(1)}, u32[]{:S(2)}, u32[]{:S(2)}) %collective-permute-start.20) | collective-permute-done | bytes 524320 | tf_op jit(solution)/shard_map/ppermute | solution.py:13
  631.9 2.8 collective-permute-start.21
  634.7 25.9 %collective-permute-done.21 = f32[512,256]{1,0:T(8,128)S(1)} collective-permute-done((f32[512,256]{1,0:T(8,128)S(1)}, f32[512,256]{1,0:T(8,128)S(1)}, u32[]{:S(2)}, u32[]{:S(2)}) %collective-permute-start.21) | collective-permute-done | bytes 524320 | tf_op jit(solution)/shard_map/ppermute | solution.py:13
  661.8 11.7 %cholesky.316 = f32[128,128]{1,0:T(8,128)S(1)} custom-call(f32[128,128]{1,0:T(8,128)S(1)} %cholesky.355), custom_call_target="Cholesky" | custom-call | tf_op jit(solution)/shard_map/jit(cholesky)/cholesky | solution.py:75
  673.6 9.8 %custom-call.23 = f32[1,128,128]{1,2,0:T(8,128)S(1)} custom-call(f32[1,128,128]{2,1,0:T(8,128)S(1)} %get-tuple-element.106), custom_call_target="InvertDiagBlocksLowerTriangular" | custom-call | tf_op jit(solution)/shard_map/jit(cholesky)/cholesky | solution.py:75
  683.9 11.7 %cholesky.333 = f32[128,128]{1,0:T(8,128)S(1)} custom-call(f32[128,128]{1,0:T(8,128)S(1)} %slice_subtract_fusion.10), custom_call_target="Cholesky" | custom-call | tf_op jit(solution)/shard_map/jit(cholesky)/cholesky | solution.py:75
  698.3 4.2 while.11
  702.6 19.7 %custom-call.24 = f32[2,128,128]{1,2,0:T(8,128)S(1)} custom-call(f32[2,128,128]{2,1,0:T(8,128)S(1)} %get-tuple-element.36), custom_call_target="InvertDiagBlocksLowerTriangular" | custom-call | tf_op jit(solution)/shard_map/jit(_solve_triangular)/triangular_solve | solution.py:77
  (205 shorter events, 112.6 us)
Async XLA Ops:
  5.3 8.1 %copy-start = (bf16[256,8,128]{2,1,0:T(8,128)(2,1)}, bf16[256,8,128]{2,1,0:T(8,128)(2,1)S(1)}, u32[]{:S(2)}) copy-start(bf16[256,8,128]{2,1,0:T(8,128)(2,1)S(1)} %gather_fusion) | copy-start | bytes 1572868
  5.9 7.6 %collective-permute-start.1 = (bf16[256,1,128]{2,1,0:T(2,128)(2,1)S(1)}, bf16[256,1,128]{2,1,0:T(2,128)(2,1)S(1)}, u32[]{:S(2)}, u32[]{:S(2)}) collective-permute-start(bf16[256,1,128]{2,1,0:T(2,128)(2,1)S(1)} %get-tuple-element.102), channel_id=1, source_target_pairs={{1,0},{2,1},{3,2},{4,3},{5,4},{6,5},{7,6},{8,7},{9,8},{10,9},{11,1... | collective-permute-start | bytes 196616 | tf_op jit(solution)/shard_map/ppermute | solution.py:32
  11.0 3.9 collective-permute-start
  16.5 17.1 %collective-permute-start.2 = (bf16[256,10,128]{2,0,1:T(8,128)(2,1)}, bf16[256,10,128]{2,0,1:T(8,128)(2,1)}, u32[]{:S(2)}, u32[]{:S(2)}) collective-permute-start(bf16[256,10,128]{2,0,1:T(8,128)(2,1)} %copy.45), channel_id=1, source_target_pairs={{0,16},{16,0},{32,48},{48,32},{64,80},{80,64},{96,112},{112,96},{1... | collective-permute-start | bytes 1966088 | tf_op jit(solution)/shard_map/ppermute | solution.py:40
  20.6 4.3 copy-start.16
  20.6 4.3 copy-start.17
  44.4 2.4 copy-start.1
  44.4 2.4 copy-start.2
  44.4 2.6 copy-start.3
  44.4 2.9 copy-start.4
  44.4 3.3 copy-start.5
  47.7 3.0 copy-start.6
  53.0 1.9 copy-start.7
  58.7 2.0 collective-permute-start.3
  60.9 13.2 %collective-permute-start.4 = (f32[512,256]{1,0:T(8,128)S(1)}, f32[512,256]{1,0:T(8,128)S(1)}, u32[]{:S(2)}, u32[]{:S(2)}) collective-permute-start(f32[512,256]{1,0:T(8,128)S(1)} %fusion.128), channel_id=1, source_target_pairs={{0,2},{1,3},{2,0},{3,1},{4,6},{5,7},{6,4},{7,5},{8,10},{9,11},{10,... | collective-permute-start | bytes 1572872 | tf_op jit(solution)/shard_map/ppermute | solution.py:13
  74.1 27.5 %collective-permute-start.5 = (f32[512,256]{1,0:T(8,128)S(1)}, f32[512,256]{1,0:T(8,128)S(1)}, u32[]{:S(2)}, u32[]{:S(2)}) collective-permute-start(f32[512,256]{1,0:T(8,128)S(1)} %add.129), channel_id=1, source_target_pairs={{0,4},{1,5},{2,6},{3,7},{4,0},{5,1},{6,2},{7,3},{8,12},{9,13},{10,... | collective-permute-start | bytes 1572872 | tf_op jit(solution)/shard_map/ppermute | solution.py:13
  101.7 27.7 %collective-permute-start.6 = (f32[512,256]{1,0:T(8,128)S(1)}, f32[512,256]{1,0:T(8,128)S(1)}, u32[]{:S(2)}, u32[]{:S(2)}) collective-permute-start(f32[512,256]{1,0:T(8,128)S(1)} %add.130), channel_id=1, source_target_pairs={{0,8},{1,9},{2,10},{3,11},{4,12},{5,13},{6,14},{7,15},{8,0},{9,1},... | collective-permute-start | bytes 1572872 | tf_op jit(solution)/shard_map/ppermute | solution.py:13
  191.5 1.6 copy-start.8
  194.1 2.9 copy-start.15
  194.1 35.6 %collective-permute-start.7 = (bf16[256,3072]{1,0:T(8,128)(2,1)S(1)}, bf16[256,3072]{1,0:T(8,128)(2,1)}, u32[]{:S(2)}, u32[]{:S(2)}) collective-permute-start(bf16[256,3072]{1,0:T(8,128)(2,1)S(1)} %convolution_convert_fusion.2), channel_id=1, source_target_pairs={{0,32},{16,48},{32,0},{48,16},{64,96},{80,112},{96,64},{112,80},{1... | collective-permute-start | bytes 4718600 | tf_op jit(solution)/shard_map/ppermute | solution.py:40
  231.8 1.8 copy-start.11
  233.7 4.5 collective-permute-start.8
  238.4 13.2 %collective-permute-start.9 = (f32[512,256]{1,0:T(8,128)S(1)}, f32[512,256]{1,0:T(8,128)S(1)}, u32[]{:S(2)}, u32[]{:S(2)}) collective-permute-start(f32[512,256]{1,0:T(8,128)S(1)} %fusion.127), channel_id=1, source_target_pairs={{0,2},{1,3},{2,0},{3,1},{4,6},{5,7},{6,4},{7,5},{8,10},{9,11},{10,... | collective-permute-start | bytes 1572872 | tf_op jit(solution)/shard_map/ppermute | solution.py:13
  251.6 25.6 %collective-permute-start.10 = (f32[512,256]{1,0:T(8,128)S(1)}, f32[512,256]{1,0:T(8,128)S(1)}, u32[]{:S(2)}, u32[]{:S(2)}) collective-permute-start(f32[512,256]{1,0:T(8,128)S(1)} %add.134), channel_id=1, source_target_pairs={{0,4},{1,5},{2,6},{3,7},{4,0},{5,1},{6,2},{7,3},{8,12},{9,13},{10,... | collective-permute-start | bytes 1572872 | tf_op jit(solution)/shard_map/ppermute | solution.py:13
  277.3 28.9 %collective-permute-start.11 = (f32[512,256]{1,0:T(8,128)S(1)}, f32[512,256]{1,0:T(8,128)S(1)}, u32[]{:S(2)}, u32[]{:S(2)}) collective-permute-start(f32[512,256]{1,0:T(8,128)S(1)} %add.135), channel_id=1, source_target_pairs={{0,8},{1,9},{2,10},{3,11},{4,12},{5,13},{6,14},{7,15},{8,0},{9,1},... | collective-permute-start | bytes 1572872 | tf_op jit(solution)/shard_map/ppermute | solution.py:13
  368.0 1.6 copy-start.12
  371.8 35.4 %collective-permute-start.12 = (bf16[256,3072]{1,0:T(8,128)(2,1)}, bf16[256,3072]{1,0:T(8,128)(2,1)}, u32[]{:S(2)}, u32[]{:S(2)}) collective-permute-start(bf16[256,3072]{1,0:T(8,128)(2,1)} %convolution_convert_fusion.1), channel_id=1, source_target_pairs={{0,64},{16,80},{32,96},{48,112},{64,0},{80,16},{96,32},{112,48},{1... | collective-permute-start | bytes 4718600 | tf_op jit(solution)/shard_map/ppermute | solution.py:40
  409.3 1.8 copy-start.13
  411.2 3.3 collective-permute-start.13
  414.6 13.2 %collective-permute-start.14 = (f32[512,256]{1,0:T(8,128)S(1)}, f32[512,256]{1,0:T(8,128)S(1)}, u32[]{:S(2)}, u32[]{:S(2)}) collective-permute-start(f32[512,256]{1,0:T(8,128)S(1)} %fusion.126), channel_id=1, source_target_pairs={{0,2},{1,3},{2,0},{3,1},{4,6},{5,7},{6,4},{7,5},{8,10},{9,11},{10,... | collective-permute-start | bytes 1572872 | tf_op jit(solution)/shard_map/ppermute | solution.py:13
  427.9 25.4 %collective-permute-start.15 = (f32[512,256]{1,0:T(8,128)S(1)}, f32[512,256]{1,0:T(8,128)S(1)}, u32[]{:S(2)}, u32[]{:S(2)}) collective-permute-start(f32[512,256]{1,0:T(8,128)S(1)} %add.139), channel_id=1, source_target_pairs={{0,4},{1,5},{2,6},{3,7},{4,0},{5,1},{6,2},{7,3},{8,12},{9,13},{10,... | collective-permute-start | bytes 1572872 | tf_op jit(solution)/shard_map/ppermute | solution.py:13
  453.3 29.2 %collective-permute-start.16 = (f32[512,256]{1,0:T(8,128)S(1)}, f32[512,256]{1,0:T(8,128)S(1)}, u32[]{:S(2)}, u32[]{:S(2)}) collective-permute-start(f32[512,256]{1,0:T(8,128)S(1)} %add.140), channel_id=1, source_target_pairs={{0,8},{1,9},{2,10},{3,11},{4,12},{5,13},{6,14},{7,15},{8,0},{9,1},... | collective-permute-start | bytes 1572872 | tf_op jit(solution)/shard_map/ppermute | solution.py:13
  544.4 1.6 copy-start.14
  548.1 37.3 %collective-permute-start.17 = (bf16[256,3072]{1,0:T(8,128)(2,1)}, bf16[256,3072]{1,0:T(8,128)(2,1)}, u32[]{:S(2)}, u32[]{:S(2)}) collective-permute-start(bf16[256,3072]{1,0:T(8,128)(2,1)} %convolution_convert_fusion), channel_id=1, source_target_pairs={{0,128},{16,144},{32,160},{48,176},{64,192},{80,208},{96,224},{112... | collective-permute-start | bytes 4718600 | tf_op jit(solution)/shard_map/ppermute | solution.py:40
  587.5 1.8 copy-start.9
  589.4 3.0 collective-permute-start.18
  592.5 13.2 %collective-permute-start.19 = (f32[512,256]{1,0:T(8,128)S(1)}, f32[512,256]{1,0:T(8,128)S(1)}, u32[]{:S(2)}, u32[]{:S(2)}) collective-permute-start(f32[512,256]{1,0:T(8,128)S(1)} %fusion.125), channel_id=1, source_target_pairs={{0,2},{1,3},{2,0},{3,1},{4,6},{5,7},{6,4},{7,5},{8,10},{9,11},{10,... | collective-permute-start | bytes 1572872 | tf_op jit(solution)/shard_map/ppermute | solution.py:13
  605.8 26.1 %collective-permute-start.20 = (f32[512,256]{1,0:T(8,128)S(1)}, f32[512,256]{1,0:T(8,128)S(1)}, u32[]{:S(2)}, u32[]{:S(2)}) collective-permute-start(f32[512,256]{1,0:T(8,128)S(1)} %add.144), channel_id=1, source_target_pairs={{0,4},{1,5},{2,6},{3,7},{4,0},{5,1},{6,2},{7,3},{8,12},{9,13},{10,... | collective-permute-start | bytes 1572872 | tf_op jit(solution)/shard_map/ppermute | solution.py:13
  631.9 28.7 %collective-permute-start.21 = (f32[512,256]{1,0:T(8,128)S(1)}, f32[512,256]{1,0:T(8,128)S(1)}, u32[]{:S(2)}, u32[]{:S(2)}) collective-permute-start(f32[512,256]{1,0:T(8,128)S(1)} %add.145), channel_id=1, source_target_pairs={{0,8},{1,9},{2,10},{3,11},{4,12},{5,13},{6,14},{7,15},{8,0},{9,1},... | collective-permute-start | bytes 1572872 | tf_op jit(solution)/shard_map/ppermute | solution.py:13
  722.2 1.6 copy-start.10
